TPU v7x, 128 devices: a whole 4x4x4 slice. The times are simulated.
128 devices in a mesh: group: 16 (over x, z), mp: 8 (over y, core).
Axes of the slice: x: 4, y: 4, z: 4, core: 2. Of those that a mesh axis runs over, the one named last changes fastest.
Arguments:
- stream: bfloat16 [8192, 3584], P('group', 'mp'), may hold values from -6 to 6
- prenorm_gain: float32 [3584], replicated, may hold values from 0.25 to 12
- query_weight: bfloat16 [3584, 4096], P(None, 'mp'), may hold values from -0.09375 to 0.09375
- key_weight: bfloat16 [3584, 2048], P(None, 'mp'), may hold values from -0.09375 to 0.09375
- value_weight: bfloat16 [3584, 2048], P(None, 'mp'), may hold values from -0.09375 to 0.09375
- output_weight: bfloat16 [4096, 3584], P('mp'), may hold values from -0.09375 to 0.09375
- adapter_down_rows: bfloat16 [64, 16, 3584], P('group', None, 'mp'), may hold values from -0.09375 to 0.09375
- adapter_up_query: bfloat16 [64, 16, 4096], P('group', None, 'mp'), may hold values from -1.5 to 1.5
- request_adapter: int32 [16, 4], replicated, may hold values from 0 to 63
- adapter_row_index: int32 [64], replicated, may hold values from 0 to 63, each once
- request_token_length: int32 [16, 4], replicated, may hold values from 1 to 256, 512 in all within a row
- continues_previous: int32 [16], replicated, may hold values from 0 to 1, as said below
- request_cache_block: int32 [16, 4], replicated, may hold values from 0 to 31, as said below
- cached_length: int32 [16, 4], replicated, may hold values from 1 to 256
- cached_rotated_keys: bfloat16 [32, 256, 2048], P('group', None, 'mp'), may hold values from -6 to 6
- cached_value_rows: bfloat16 [32, 256, 2048], P('group', None, 'mp'), may hold values from -6 to 6
Outputs:
- attn_out: bfloat16 [8192, 3584], P('group', 'mp')
Inputs may be any that keep to these rules, and one draw needn't show every extreme that they name: `continues_previous`: the first group has 0; some group has 1. `request_cache_block`: the owner of block b is group b // 2; blocks may be shared by requests.
All inputs are finite; a program needn't handle non-finite values.
Results may differ from a plain program's by a relative error of at most 0.017.
The roundings to bfloat16 on the way count: a program that leaves them out, or rounds other values in their place, can miss the bound.
Values may be sent and summed in bfloat16 or wider, within the bound.
No kernel may reach another device: no remote copies, remote signals or barrier semaphores. Data moves between devices by JAX's collectives and lax.ppermute only.
A program may use at most 128 MiB of HBM per device.

v0:
```python
import jax
import jax.numpy as jnp
from jax import lax
from jax.sharding import PartitionSpec as P

HEAD_WIDTH = 256
REQS = 4
adapter_scale = 2.0


def shifted(value, axis, steps):
    count = lax.axis_size(axis)
    first, last = (max(0, -steps), min(count, count - steps))
    return lax.ppermute(value, axis, [(source, source + steps) for source in range(first, last)])


def rotate(values, position, head_size):
    count = values.shape[0]
    shaped = values.reshape(count, -1, head_size)
    half = head_size // 2
    freq = 10000.0 ** (-jnp.arange(half, dtype=jnp.float32) / half)
    angle = position[:, None, None] * freq[None, None, :]
    cosine = jnp.cos(angle)
    sine = jnp.sin(angle)
    first = shaped[..., :half]
    second = shaped[..., half:]
    turned = jnp.concatenate(
        [first * cosine - second * sine, second * cosine + first * sine], axis=-1
    )
    return turned.reshape(count, -1)


def layout(lengths, cached, split_flag, prev_len, count):
    ends = jnp.cumsum(lengths)
    starts = ends - lengths
    place = jnp.arange(count, dtype=jnp.int32)
    member = ((place[:, None] >= starts[None, :]) & (place[:, None] < ends[None, :])).astype(
        jnp.int32
    )
    request = jnp.sum(member * jnp.arange(lengths.shape[0], dtype=jnp.int32)[None, :], axis=1)
    offset = place - jnp.sum(member * starts[None, :], axis=1)
    extra = jnp.where(request == 0, split_flag * prev_len, 0)
    position = jnp.sum(member * cached[None, :], axis=1) + extra + offset
    return (member, request, position.astype(jnp.float32))


def attend(
    query_vectors,
    keys,
    values,
    prev_keys,
    prev_values,
    cache_keys,
    cache_values,
    request,
    cached,
    split_flag,
    prev_len,
    head_size,
):
    count = query_vectors.shape[0]
    kv_heads = keys.shape[1] // head_size
    ratio = query_vectors.shape[1] // keys.shape[1]
    block = cache_keys.shape[1]
    slots = cache_keys.shape[0] * block
    every_key = jnp.concatenate([cache_keys.reshape(slots, -1), prev_keys, keys], 0).reshape(
        -1, kv_heads, head_size
    )
    every_value = jnp.concatenate(
        [cache_values.reshape(slots, -1), prev_values, values], 0
    ).reshape(-1, kv_heads, head_size)
    slot_req = jnp.arange(slots, dtype=jnp.int32) // block
    slot_col = jnp.arange(slots, dtype=jnp.int32) % block
    cache_ok = (request[:, None] == slot_req[None, :]) & (
        slot_col[None, :] < cached[slot_req][None, :]
    )
    place = jnp.arange(count, dtype=jnp.int32)
    prev_ok = (split_flag == 1) & (request[:, None] == 0) & (place[None, :] >= count - prev_len)
    own_ok = (request[:, None] == request[None, :]) & (place[None, :] <= place[:, None])
    allowed = jnp.concatenate([cache_ok, prev_ok, own_ok], 1)
    grouped = query_vectors.reshape(count, kv_heads, ratio, head_size)
    scores = jnp.einsum(
        "tkrd,skd->krts", grouped, every_key, preferred_element_type=jnp.float32
    ) * head_size ** (-0.5)
    scores = jnp.where(allowed[None, None], scores, jnp.float32(-1e30))
    top = jnp.max(scores, axis=-1, keepdims=True)
    weights = jnp.exp(scores - top)
    total = jnp.sum(weights, axis=-1)
    numer = jnp.einsum(
        "krts,skd->tkrd",
        weights.astype(jnp.bfloat16),
        every_value,
        preferred_element_type=jnp.float32,
    )
    result = numer / jnp.transpose(total, (2, 0, 1))[..., None]
    return result.reshape(count, -1).astype(jnp.bfloat16)


def on_device(
    stream,
    prenorm_gain,
    query_weight,
    key_weight,
    value_weight,
    output_weight,
    adapter_down_rows,
    adapter_up_query,
    request_adapter,
    adapter_row_index,
    request_token_length,
    continues_previous,
    request_cache_block,
    cached_length,
    cached_rotated_keys,
    cached_value_rows,
):
    count = stream.shape[0]
    width = stream.shape[1]
    group_at = lax.axis_index("group")
    model_at = lax.axis_index("mp")
    whole = lax.all_gather(stream, "mp", axis=1, tiled=True)
    wide = whole.astype(jnp.float32)
    normalized_input = (
        wide * lax.rsqrt(jnp.mean(wide * wide, axis=1, keepdims=True) + 1e-06) * prenorm_gain
    ).astype(jnp.bfloat16)
    normed_part = lax.dynamic_slice_in_dim(normalized_input, model_at * width, width, 1)
    before = jnp.maximum(group_at - 1, 0)
    lengths = request_token_length[group_at]
    cached = cached_length[group_at]
    split_flag = continues_previous[group_at]
    prev_len = request_token_length[before, REQS - 1]
    member, request, position = layout(lengths, cached, split_flag, prev_len, count)
    wanted = adapter_row_index[request_adapter[group_at]]
    pieces = (
        lax.all_gather(adapter_down_rows, "group", axis=0, tiled=True),
        lax.all_gather(adapter_up_query, "group", axis=0, tiled=True),
    )
    stored = jnp.arange(pieces[0].shape[0], dtype=jnp.int32)
    onehot = (wanted[:, None] == stored[None, :]).astype(jnp.bfloat16)
    new_down = jnp.einsum("rj,jkd->rkd", onehot, pieces[0], preferred_element_type=jnp.float32)
    new_up = jnp.einsum("rj,jkd->rkd", onehot, pieces[1], preferred_element_type=jnp.float32)
    chosen_down = new_down.astype(jnp.bfloat16)
    chosen_up = new_up.astype(jnp.bfloat16)
    rank_index = adapter_down_rows.shape[1]
    partial_low = jnp.einsum(
        "td,rkd->trk", normed_part, chosen_down, preferred_element_type=jnp.float32
    ).reshape(count, REQS * rank_index)
    low = lax.psum(partial_low, "mp").astype(jnp.bfloat16)
    own_columns = jnp.repeat(member, rank_index, axis=1).astype(jnp.bfloat16)
    query_update = jnp.dot(
        low * own_columns,
        chosen_up.reshape(REQS * rank_index, -1),
        preferred_element_type=jnp.float32,
    )
    query_vectors = (
        jnp.dot(normalized_input, query_weight, preferred_element_type=jnp.float32)
        + adapter_scale * query_update
    )
    query_vectors = rotate(query_vectors, position, HEAD_WIDTH).astype(jnp.bfloat16)
    keys = rotate(
        jnp.dot(normalized_input, key_weight, preferred_element_type=jnp.float32),
        position,
        HEAD_WIDTH,
    ).astype(jnp.bfloat16)
    values = jnp.dot(normalized_input, value_weight, preferred_element_type=jnp.float32).astype(
        jnp.bfloat16
    )
    prev_keys, prev_values = shifted((keys, values), "group", 1)
    blocks = request_cache_block[group_at]
    pieces = (
        lax.all_gather(cached_rotated_keys, "group", axis=0, tiled=True),
        lax.all_gather(cached_value_rows, "group", axis=0, tiled=True),
    )
    stored = jnp.arange(pieces[0].shape[0], dtype=jnp.int32)
    onehot = (blocks[:, None] == stored[None, :]).astype(jnp.bfloat16)
    new_keys = jnp.einsum("rj,jcd->rcd", onehot, pieces[0], preferred_element_type=jnp.float32)
    new_values = jnp.einsum("rj,jcd->rcd", onehot, pieces[1], preferred_element_type=jnp.float32)
    cache_keys = new_keys.astype(jnp.bfloat16)
    cache_values = new_values.astype(jnp.bfloat16)
    attended = attend(
        query_vectors,
        keys,
        values,
        prev_keys,
        prev_values,
        cache_keys,
        cache_values,
        request,
        cached,
        split_flag,
        prev_len,
        HEAD_WIDTH,
    )
    partial_out = jnp.dot(attended, output_weight, preferred_element_type=jnp.float32)
    return lax.psum_scatter(partial_out.astype(jnp.bfloat16), "mp", scatter_dimension=1, tiled=True)


def solution(mesh):
    placed = (
        P("group", "mp"),
        P(),
        P(None, "mp"),
        P(None, "mp"),
        P(None, "mp"),
        P("mp", None),
        P("group", None, "mp"),
        P("group", None, "mp"),
        P(),
        P(),
        P(),
        P(),
        P(),
        P(),
        P("group", None, "mp"),
        P("group", None, "mp"),
    )
    return jax.shard_map(
        on_device, mesh=mesh, in_specs=placed, out_specs=P("group", "mp"), check_vma=False
    )
```

profile of v0, /device:TPU:0, one launch (start us, length us, event | category | flops | bytes accessed | tf_op | source)
XLA Modules:
  0.0 254.0 jit_solution(16617972660007501374)
XLA Ops:
  6.5 0.7 all-gather.11.cloned.1.call-update
  7.3 0.0 all-gather.7.cloned.1.call-start
  7.3 0.7 all-gather.7.cloned.1.call-update
  8.0 0.0 all-gather.5.cloned.1.call-start
  8.1 0.7 all-gather.5.cloned.1.call-update
  8.7 0.0 all-gather.9.cloned.1.call-start
  8.8 0.5 all-gather.9.cloned.1.call-update
  9.3 0.0 reduce-scatter.2.cloned.1.call-start
  9.4 1.3 constant_dynamic-slice_fusion.2
  10.7 0.9 dynamic-slice_reduce_fusion
  11.6 0.1 copy.61
  11.7 0.2 reduce-window.4
  11.9 0.9 fusion.79
  12.8 0.6 fusion.81
  13.4 26.9 %all_gather.18 = bf16[64,16,448]{2,1,0:T(8,128)(2,1)S(1)} all-gather(bf16[4,16,448]{2,1,0:T(8,128)(2,1)} %param.22), channel_id=1, replica_groups=mesh['group'=16,'mp'=8] {'group'}, dimensions={0}, use_global_device_ids=true | all-gather | bytes 974848 | tf_op jit(solution)/shard_map/all_gather | solution.py:135
  40.9 2.6 %compare_select_fusion.1 = s32[1024,1]{0,1:T(1,128)S(1)} fusion(s32[]{:T(128)} %bitcast.7, s32[]{:T(128)} %bitcast.8, s32[]{:T(128)} %bitcast.10, s32[]{:T(128)} %bitcast.9), kind=kLoop, calls=%fused_computation.71 | loop fusion | flops 17408 | bytes 4112 | tf_op jit(solution)/shard_map/gather | solution.py:75
  43.5 1.2 dynamic_slice.24
  46.8 0.9 dynamic-slice_reduce_fusion.1
  47.6 1.3 gather_fusion
  48.9 0.1 select_reduce_fusion.2
  49.0 0.1 convert_convert_fusion
  49.1 0.2 broadcast_and_fusion
  49.3 0.2 fusion.35
  49.5 1.8 multiply_cosine_fusion
  51.4 0.8 compare_and_fusion
  52.2 1.2 convolution_convert_fusion.3
  53.4 0.4 pad_add_fusion
  53.8 1.2 all-gather.11.cloned.1.call-done
  54.9 2.4 convolution_convert_fusion.2
  57.4 28.5 %all-gather.7.cloned.1.call-done = bf16[512,3584]{0,1:T(8,128)(2,1)} async-done(((bf16[512,448]{0,1:T(8,128)(2,1)}), bf16[512,3584]{0,1:T(8,128)(2,1)}) %all-gather.7.cloned.1.call-update) | async-done | bytes 3670032 | tf_op jit(solution)/shard_map/all_gather | solution.py:121
  85.8 3.0 %fusion.2 = f32[512]{0:T(512)S(1)} fusion(bf16[512,3584]{0,1:T(8,128)(2,1)} %all-gather.7.cloned.1.call-done), kind=kLoop, calls=%fused_computation.7 | loop fusion | flops 5504512 | bytes 3672064 | tf_op jit(solution)/shard_map/reduce_sum | solution.py:124
  88.9 0.1 copy-done.1
  89.0 1.6 fusion.4
  90.6 1.8 copy-done.2
  92.4 1.9 convolution_convert_fusion.1
  94.3 1.8 copy.47
  96.1 4.2 %collective-permute-start = (bf16[512,256]{1,0:T(8,128)(2,1)}, bf16[512,256]{1,0:T(8,128)(2,1)}, u32[]{:S(2)}, u32[]{:S(2)}) collective-permute-start(bf16[512,256]{1,0:T(8,128)(2,1)} %convolution_convert_fusion.1), channel_id=1, source_target_pairs={{0,8},{8,16},{16,24},{24,32},{32,40},{40,48},{48,56},{56,64},{64,7... | collective-permute-start | bytes 786440 | tf_op jit(solution)/shard_map/ppermute | solution.py:14
  100.2 3.8 %convolution_bitcast_fusion = f32[512,1,256]{0,2,1:T(8,128)S(1)} fusion(bf16[512,3584]{0,1:T(8,128)(2,1)} %copy-done.2, bf16[3584,256]{1,0:T(8,128)(2,1)} %param.19), kind=kOutput, calls=%fused_computation.26 | convolution fusion | flops 939524096 | bytes 6029312 | tf_op jit(solution)/shard_map/dot_general | solution.py:161
  104.0 1.2 fusion.49
  105.2 0.7 maximum_bitcast_fusion.6
  105.9 1.8 copy.52
  107.7 3.4 %collective-permute-start.1 = (bf16[512,256]{0,1:T(8,128)(2,1)}, bf16[512,256]{0,1:T(8,128)(2,1)}, u32[]{:S(2)}, u32[]{:S(2)}) collective-permute-start(bf16[512,256]{0,1:T(8,128)(2,1)} %maximum_bitcast_fusion.6), channel_id=1, source_target_pairs={{0,8},{8,16},{16,24},{24,32},{32,40},{40,48},{48,56},{56,64},{64,7... | collective-permute-start | bytes 786440 | tf_op jit(solution)/shard_map/ppermute | solution.py:14
  111.1 1.2 fusion.41
  112.3 26.0 %all-reduce.1 = bf16[512,64]{0,1:T(8,128)(2,1)S(1)} all-reduce(f32[512,64]{0,1:T(8,128)S(1)} %bitcast.101), channel_id=1, replica_groups=mesh['group'=16,'mp'=8] {'mp'}, use_global_device_ids=true, to_apply=%region_5.6 | all-reduce | flops 32768 | bytes 196608 | tf_op jit(solution)/shard_map/psum | solution.py:148
  138.4 5.3 %fusion.82 = f32[512,512]{0,1:T(8,128)S(1)} fusion(bf16[512,3584]{0,1:T(8,128)(2,1)} %copy-done.2, bf16[3584,512]{1,0:T(8,128)(2,1)} %param.18), kind=kOutput, calls=%fused_computation.129 | convolution fusion | flops 1879048192 | bytes 8388608 | tf_op jit(solution)/shard_map/dot_general | solution.py:156
  143.7 0.3 fusion.17
  144.0 1.1 fusion.80
  145.1 1.2 copy.63
  146.4 2.1 copy.62
  148.5 2.2 subtract_convert_fusion
  150.6 1.8 copy.46
  152.5 1.8 copy.51
  154.3 4.6 %fusion.18 = bf16[4,256,256]{2,0,1:T(4,128)(2,1)S(1)} fusion(bf16[32,256,256]{2,1,0:T(8,128)(2,1)} %all-gather.5.cloned.1.call-done, s32[4]{0:T(128)S(1)} %dynamic-slice_reduce_fusion.1), kind=kOutput, calls=%fused_computation.24 | convolution fusion | flops 17039488 | bytes 4718608 | tf_op jit(solution)/shard_map/rj,jcd->rcd/dot_general | solution.py:177
  158.9 0.1 copy.44
  159.0 1.0 copy.45
  160.0 35.3 %all-gather.9.cloned.1.call-done = bf16[32,256,256]{2,1,0:T(8,128)(2,1)} async-done(((bf16[2,256,256]{2,1,0:T(8,128)(2,1)}), bf16[32,256,256]{2,1,0:T(8,128)(2,1)}) %all-gather.9.cloned.1.call-update) | async-done | bytes 4194320 | tf_op jit(solution)/shard_map/all_gather | solution.py:171
  195.3 4.7 %fusion.21 = bf16[4,256,256]{2,0,1:T(4,128)(2,1)S(1)} fusion(bf16[32,256,256]{2,1,0:T(8,128)(2,1)} %all-gather.9.cloned.1.call-done, s32[4]{0:T(128)S(1)} %dynamic-slice_reduce_fusion.1), kind=kOutput, calls=%fused_computation.25 | convolution fusion | flops 17039488 | bytes 4718608 | tf_op jit(solution)/shard_map/rj,jcd->rcd/dot_general | solution.py:176
  200.0 0.1 copy.50
  200.1 1.8 fusion.5
  201.9 2.2 fusion
  204.2 2.8 %divide_convert_fusion = bf16[512,1,2,256]{0,3,2,1:T(8,128)(2,1)S(1)} fusion(f32[2048,512,2]{1,0,2:T(8,128)S(1)} %get-tuple-element.25, f32[2,512]{1,0:T(2,128)S(1)} %get-tuple-element.24, pred[512,2048]{0,1:T(8,128)(4,1)S(1)} %pad_add_fusion, bf16[512,256]{0,1:T(8,128)(2,1)S(1)} %copy-done.4, bf16[512,256]{0,1:T(8,128)(2,1)S(1)} %copy-done.6, ...), kind=kOutput, calls=%fused_computation.43 | convolution fusion | flops 1085800448 | bytes 11018240 | tf_op jit(solution)/shard_map/krts,skd->tkrd/dot_general | solution.py:89
  207.0 3.9 %convolution_convert_fusion = bf16[512,3584]{0,1:T(8,128)(2,1)} fusion(bf16[512,512]{0,1:T(8,128)(2,1)S(1)} %bitcast.107, bf16[512,3584]{1,0:T(8,128)(2,1)S(1)} %copy-done.11), kind=kOutput, calls=%fused_computation.11 | convolution fusion | flops 1880883200 | bytes 7864320 | tf_op jit(solution)/shard_map/dot_general | solution.py:194
  210.9 0.0 reduce-scatter.2.cloned.1.call-update
  210.9 36.5 %reduce-scatter.2.cloned.1.call-done = bf16[512,448]{0,1:T(8,128)(2,1)} async-done(((bf16[512,3584]{0,1:T(8,128)(2,1)}), bf16[512,448]{0,1:T(8,128)(2,1)}) %reduce-scatter.2.cloned.1.call-update) | async-done | bytes 458768 | tf_op jit(solution)/shard_map/reduce_scatter | solution.py:195
  (38 shorter events, 0.2 us)
Async XLA Ops:
  6.5 85.8 %copy-start = (bf16[3584,256]{1,0:T(8,128)(2,1)S(1)}, bf16[3584,256]{1,0:T(8,128)(2,1)}, u32[]{:S(2)}) copy-start(bf16[3584,256]{1,0:T(8,128)(2,1)} %param.20) | copy-start | bytes 5505028
  6.5 48.4 %all-gather.11.cloned.1.call-start = ((), (), s32[]{:S(2)}) async-start(), calls=%async_computation.4 | async-start | bytes 1114112 | tf_op jit(solution)/shard_map/all_gather | solution.py:136
  7.3 78.6 %all-gather.7.cloned.1.call-start = ((), (), s32[]{:S(2)}) async-start(), calls=%async_computation.2 | async-start | bytes 4128768 | tf_op jit(solution)/shard_map/all_gather | solution.py:121
  8.0 146.3 %all-gather.5.cloned.1.call-start = ((), (), s32[]{:S(2)}) async-start(), calls=%async_computation.1 | async-start | bytes 4456448 | tf_op jit(solution)/shard_map/all_gather | solution.py:172
  8.7 186.5 %all-gather.9.cloned.1.call-start = ((), (), s32[]{:S(2)}) async-start(), calls=%async_computation.3 | async-start | bytes 4456448 | tf_op jit(solution)/shard_map/all_gather | solution.py:171
  9.3 238.1 %reduce-scatter.2.cloned.1.call-start = ((), (), s32[]{:S(2)}) async-start(), calls=%async_computation.5 | async-start | bytes 4128768 | tf_op jit(solution)/shard_map/reduce_scatter | solution.py:195
  53.4 35.5 %copy-start.10 = (f32[3584]{0:T(1024)S(1)}, f32[3584]{0:T(1024)}, u32[]{:S(2)}) copy-start(f32[3584]{0:T(1024)} %param.17) | copy-start | bytes 43012
  85.8 3.1 %copy-start.1 = (bf16[512,3584]{0,1:T(8,128)(2,1)S(1)}, bf16[512,3584]{0,1:T(8,128)(2,1)}, u32[]{:S(2)}) copy-start(bf16[512,3584]{0,1:T(8,128)(2,1)} %all-gather.7.cloned.1.call-done) | copy-start | bytes 11010052
  90.5 1.8 copy-start.2
  96.1 54.6 %collective-permute-start = (bf16[512,256]{1,0:T(8,128)(2,1)}, bf16[512,256]{1,0:T(8,128)(2,1)}, u32[]{:S(2)}, u32[]{:S(2)}) collective-permute-start(bf16[512,256]{1,0:T(8,128)(2,1)} %convolution_convert_fusion.1), channel_id=1, source_target_pairs={{0,8},{8,16},{16,24},{24,32},{32,40},{40,48},{48,56},{56,64},{64,7... | collective-permute-start | bytes 786440 | tf_op jit(solution)/shard_map/ppermute | solution.py:14
  107.7 44.8 %collective-permute-start.1 = (bf16[512,256]{0,1:T(8,128)(2,1)}, bf16[512,256]{0,1:T(8,128)(2,1)}, u32[]{:S(2)}, u32[]{:S(2)}) collective-permute-start(bf16[512,256]{0,1:T(8,128)(2,1)} %maximum_bitcast_fusion.6), channel_id=1, source_target_pairs={{0,8},{8,16},{16,24},{24,32},{32,40},{40,48},{48,56},{56,64},{64,7... | collective-permute-start | bytes 786440 | tf_op jit(solution)/shard_map/ppermute | solution.py:14
  160.0 40.1 %copy-start.5 = (bf16[512,256]{1,0:T(8,128)(2,1)S(1)}, bf16[512,256]{1,0:T(8,128)(2,1)}, u32[]{:S(2)}) copy-start(bf16[512,256]{1,0:T(8,128)(2,1)} %copy.52) | copy-start | bytes 786436
  160.0 40.1 %copy-start.7 = (bf16[512,256]{1,0:T(8,128)(2,1)S(1)}, bf16[512,256]{1,0:T(8,128)(2,1)}, u32[]{:S(2)}) copy-start(bf16[512,256]{1,0:T(8,128)(2,1)} %copy.51) | copy-start | bytes 786436
  195.3 4.8 %copy-start.8 = (bf16[512,2,128]{2,0,1:T(8,128)(2,1)S(1)}, bf16[512,2,128]{2,0,1:T(8,128)(2,1)}, u32[]{:S(2)}) copy-start(bf16[512,2,128]{2,0,1:T(8,128)(2,1)} %get-tuple-element.12) | copy-start | bytes 786436
  195.3 4.8 %copy-start.9 = (bf16[512,2,128]{2,0,1:T(8,128)(2,1)S(1)}, bf16[512,2,128]{2,0,1:T(8,128)(2,1)}, u32[]{:S(2)}) copy-start(bf16[512,2,128]{2,0,1:T(8,128)(2,1)} %get-tuple-element.13) | copy-start | bytes 786436
  201.9 2.2 copy-start.3
  201.9 2.2 copy-start.4
  201.9 2.2 copy-start.6
  204.2 2.8 %copy-start.11 = (bf16[512,3584]{1,0:T(8,128)(2,1)S(1)}, bf16[512,3584]{1,0:T(8,128)(2,1)}, u32[]{:S(2)}) copy-start(bf16[512,3584]{1,0:T(8,128)(2,1)} %param.21) | copy-start | bytes 11010052
Sparse Core Ops, SparseCore 0:
  9.5 45.3 all-gather.10
  56.6 29.1 all-gather.6
  88.0 53.9 all-gather.4
  144.0 51.2 all-gather.8
  211.0 36.3 reduce-scatter.1
where the time goes:
time: 255 us; the launch traced here: 254 us
  waiting for transfers between devices  104 us (41%)
  blocking collectives  52.9 us (21%)
  matrix products  33.9 us (13%)
  local copies, waits for them, and re-layouts  21.9 us (9%)
  other arithmetic  17.3 us (7%)
  between operations  16.1 us (6%)
  starting transfers between devices  7.77 us (3%)
    reduce_scatter x1, waiting for transfers between devices, on_device(): lax.psum_scatter(partial_out.astype(jnp.bfloat16), 'mp', scatter_dimensio...  36.5 us
    all_gather x1, waiting for transfers between devices, on_device(): lax.all_gather(cached_rotated_keys, 'group', axis=0, tiled=True)  35.3 us
    all_gather x1, waiting for transfers between devices, on_device(): whole = lax.all_gather(stream, 'mp', axis=1, tiled=True)  28.5 us
    all_gather x1, blocking collectives, on_device(): lax.all_gather(adapter_down_rows, 'group', axis=0, tiled=True)  26.9 us
    psum x1, blocking collectives, on_device(): low = lax.psum(partial_low, 'mp').astype(jnp.bfloat16)  26 us
    ppermute x2, starting transfers between devices, shifted(): lax.ppermute(value, axis, [(source, source + steps) for source in range(f...  7.62 us
    unnamed x27, local copies, waits for them, and re-layouts  5.37 us
    dot_general x1, matrix products, on_device(): jnp.dot(normalized_input, query_weight, preferred_element_type=jnp.float32)  5.26 us
  transfers between devices with their start and end apart: 7, of which 4 were waited for; matrix products, arithmetic and copies ran while one was open for 22% of the time, Pallas kernels for 0%

commit v1 on v0

--- a/solution.py
+++ b/solution.py
@@ -6,6 +6,13 @@
 HEAD_WIDTH = 256
 REQS = 4
 adapter_scale = 2.0
+
+
+def detail_the_grid(own_rows):
+    local_next = jnp.concatenate(
+        lax.all_to_all(jnp.stack(lax.axis_size("group") * [own_rows]), "group", 0, 0), axis=0
+    )
+    return local_next
 
 
 def shifted(value, axis, steps):
@@ -132,7 +139,7 @@
     member, request, position = layout(lengths, cached, split_flag, prev_len, count)
     wanted = adapter_row_index[request_adapter[group_at]]
     pieces = (
-        lax.all_gather(adapter_down_rows, "group", axis=0, tiled=True),
+        detail_the_grid(adapter_down_rows),
         lax.all_gather(adapter_up_query, "group", axis=0, tiled=True),
     )
     stored = jnp.arange(pieces[0].shape[0], dtype=jnp.int32)

time: 255 us -> 259 us (1.016)
  waiting for transfers between devices: 104 us -> 131 us
  blocking collectives: 52.9 us -> 26 us
  starting transfers between devices: 7.77 us -> 15.8 us
  local copies, waits for them, and re-layouts: 21.9 us -> 19.2 us
    all_gather x1 -> x0, blocking collectives: 26.9 us -> none  [on_device(): lax.all_gather(adapter_down_rows, 'group', axis=0, tiled=True)]
    all_gather x1, waiting for transfers between devices: 1.16 us -> 18.6 us  [on_device(): lax.all_gather(adapter_up_query, 'group', axis=0, tiled=True)]
    all_to_all x0 -> x1, starting transfers between devices: none -> 7.96 us  [detail_the_grid(): lax.all_to_all(jnp.stack(lax.axis_size('group') * [own_rows]), 'group', 0...]
    all_to_all x0 -> x1, waiting for transfers between devices: none -> 4.8 us  [detail_the_grid(): lax.all_to_all(jnp.stack(lax.axis_size('group') * [own_rows]), 'group', 0...]
    all_gather x1, waiting for transfers between devices: 35.3 us -> 39.5 us  [on_device(): lax.all_gather(cached_rotated_keys, 'group', axis=0, tiled=True)]
    unnamed x27 -> x42, local copies, waits for them, and re-layouts: 5.37 us -> 3.33 us
  transfers between devices with their start and end apart: 7 -> 8, of which waited for: 4 -> 5; matrix products, arithmetic and copies ran while one was open for 22% -> 20% of each run, Pallas kernels for 0% -> 0%
where the time goes in v1:
time: 259 us
  waiting for transfers between devices  131 us (51%)
  matrix products  33.1 us (13%)
  blocking collectives  26 us (10%)
  local copies, waits for them, and re-layouts  19.2 us (7%)
  other arithmetic  18 us (7%)
  between operations  16.1 us (6%)
  starting transfers between devices  15.8 us (6%)
    all_gather x1, waiting for transfers between devices, on_device(): lax.all_gather(cached_rotated_keys, 'group', axis=0, tiled=True)  39.5 us
    reduce_scatter x1, waiting for transfers between devices, on_device(): lax.psum_scatter(partial_out.astype(jnp.bfloat16), 'mp', scatter_dimensio...  36.6 us
    all_gather x1, waiting for transfers between devices, on_device(): whole = lax.all_gather(stream, 'mp', axis=1, tiled=True)  28.5 us
    psum x1, blocking collectives, on_device(): low = lax.psum(partial_low, 'mp').astype(jnp.bfloat16)  26 us
    all_gather x1, waiting for transfers between devices, on_device(): lax.all_gather(adapter_up_query, 'group', axis=0, tiled=True)  18.6 us
    all_to_all x1, starting transfers between devices, detail_the_grid(): lax.all_to_all(jnp.stack(lax.axis_size('group') * [own_rows]), 'group', 0...  7.96 us
    ppermute x2, starting transfers between devices, shifted(): lax.ppermute(value, axis, [(source, source + steps) for source in range(f...  7.61 us
    dot_general x1, matrix products, on_device(): jnp.dot(normalized_input, query_weight, preferred_element_type=jnp.float32)  5.26 us
  transfers between devices with their start and end apart: 8, of which 5 were waited for; matrix products, arithmetic and copies ran while one was open for 20% of the time, Pallas kernels for 0%

profile of v1, /device:TPU:0, one launch (start us, length us, event | category | flops | bytes accessed | tf_op | source)
XLA Modules:
  0.0 258.8 jit_solution(3310667771535436416)
XLA Ops:
  6.6 0.7 all-gather.11.cloned.1.call-update
  7.3 0.7 all-gather.7.cloned.1.call-update
  8.1 0.7 all-gather.5.cloned.1.call-update
  8.8 0.9 copy.70
  9.7 1.4 stack.2
  11.1 8.0 %all-to-all-start = ((bf16[16,4,16,448]{3,1,2,0:T(4,128)(2,1)}), bf16[16,4,16,448]{3,1,2,0:T(4,128)(2,1)S(1)}, u32[]{:S(2)}, u32[]{:S(2)}) async-start(bf16[16,4,16,448]{3,1,2,0:T(4,128)(2,1)} %stack.2), calls=%async_computation | async-start | bytes 2097152 | tf_op jit(solution)/shard_map/all_to_all | solution.py:13
  19.1 0.5 all-gather.9.cloned.1.call-update
  19.7 0.6 constant_dynamic-slice_fusion.2
  20.3 0.2 dynamic-slice_reduce_fusion
  20.5 0.1 copy.79
  20.6 0.2 reduce-window.4
  20.8 0.2 fusion.78
  21.0 0.6 fusion.80
  22.2 0.1 select_reduce_fusion.2
  22.3 2.5 compare_select_fusion.1
  24.8 0.6 dynamic_slice.24
  27.4 0.2 dynamic-slice_reduce_fusion.1
  27.5 0.6 gather_fusion
  28.2 0.1 convert_convert_fusion
  28.3 0.2 broadcast_and_fusion
  28.5 0.2 fusion.34
  28.7 1.8 multiply_cosine_fusion
  30.5 0.8 compare_and_fusion
  31.3 1.4 pad_add_fusion
  32.7 4.8 %all-to-all-done = bf16[16,4,16,448]{3,1,2,0:T(4,128)(2,1)S(1)} async-done(((bf16[16,4,16,448]{3,1,2,0:T(4,128)(2,1)}), bf16[16,4,16,448]{3,1,2,0:T(4,128)(2,1)S(1)}, u32[]{:S(2)}, u32[]{:S(2)}) %all-to-all-start) | async-done | bytes 917536 | tf_op jit(solution)/shard_map/all_to_all | solution.py:13
  37.5 1.5 copy.71
  39.0 1.6 reshape.319
  40.6 0.3 convolution_convert_fusion.3
  40.9 18.6 %all-gather.11.cloned.1.call-done = bf16[64,16,512]{2,1,0:T(8,128)(2,1)} async-done(((bf16[4,16,512]{2,1,0:T(8,128)(2,1)}), bf16[64,16,512]{2,1,0:T(8,128)(2,1)}) %all-gather.11.cloned.1.call-update) | async-done | bytes 1048592 | tf_op jit(solution)/shard_map/all_gather | solution.py:143
  59.5 2.4 convolution_convert_fusion.2
  62.0 28.5 %all-gather.7.cloned.1.call-done = bf16[512,3584]{0,1:T(8,128)(2,1)} async-done(((bf16[512,448]{0,1:T(8,128)(2,1)}), bf16[512,3584]{0,1:T(8,128)(2,1)}) %all-gather.7.cloned.1.call-update) | async-done | bytes 3670032 | tf_op jit(solution)/shard_map/all_gather | solution.py:128
  90.5 3.0 %fusion.2 = f32[512]{0:T(512)S(1)} fusion(bf16[512,3584]{0,1:T(8,128)(2,1)} %all-gather.7.cloned.1.call-done), kind=kLoop, calls=%fused_computation.7 | loop fusion | flops 5504512 | bytes 3672064 | tf_op jit(solution)/shard_map/reduce_sum | solution.py:131
  93.5 0.1 copy-done.2
  93.6 1.6 fusion.4
  95.2 1.8 copy-done.4
  97.0 1.9 convolution_convert_fusion.1
  98.9 1.8 copy.64
  100.7 4.2 %collective-permute-start = (bf16[512,256]{1,0:T(8,128)(2,1)}, bf16[512,256]{1,0:T(8,128)(2,1)}, u32[]{:S(2)}, u32[]{:S(2)}) collective-permute-start(bf16[512,256]{1,0:T(8,128)(2,1)} %convolution_convert_fusion.1), channel_id=1, source_target_pairs={{0,8},{8,16},{16,24},{24,32},{32,40},{40,48},{48,56},{56,64},{64,7... | collective-permute-start | bytes 786440 | tf_op jit(solution)/shard_map/ppermute | solution.py:21
  104.9 3.8 %convolution_bitcast_fusion = f32[512,1,256]{0,2,1:T(8,128)S(1)} fusion(bf16[512,3584]{0,1:T(8,128)(2,1)} %copy-done.4, bf16[3584,256]{1,0:T(8,128)(2,1)} %param.19), kind=kOutput, calls=%fused_computation.26 | convolution fusion | flops 939524096 | bytes 6029312 | tf_op jit(solution)/shard_map/dot_general | solution.py:168
  108.6 1.2 fusion.48
  109.8 0.7 maximum_bitcast_fusion.6
  110.6 1.8 copy.69
  112.3 3.4 %collective-permute-start.1 = (bf16[512,256]{0,1:T(8,128)(2,1)}, bf16[512,256]{0,1:T(8,128)(2,1)}, u32[]{:S(2)}, u32[]{:S(2)}) collective-permute-start(bf16[512,256]{0,1:T(8,128)(2,1)} %maximum_bitcast_fusion.6), channel_id=1, source_target_pairs={{0,8},{8,16},{16,24},{24,32},{32,40},{40,48},{48,56},{56,64},{64,7... | collective-permute-start | bytes 786440 | tf_op jit(solution)/shard_map/ppermute | solution.py:21
  115.8 1.2 fusion.40
  117.0 26.0 %all-reduce.1 = bf16[512,64]{0,1:T(8,128)(2,1)S(1)} all-reduce(f32[512,64]{0,1:T(8,128)S(1)} %bitcast.104), channel_id=1, replica_groups=mesh['group'=16,'mp'=8] {'mp'}, use_global_device_ids=true, to_apply=%region_5.6 | all-reduce | flops 32768 | bytes 196608 | tf_op jit(solution)/shard_map/psum | solution.py:155
  143.1 5.3 %fusion.81 = f32[512,512]{0,1:T(8,128)S(1)} fusion(bf16[512,3584]{0,1:T(8,128)(2,1)} %copy-done.4, bf16[3584,512]{1,0:T(8,128)(2,1)} %param.18), kind=kOutput, calls=%fused_computation.128 | convolution fusion | flops 1879048192 | bytes 8388608 | tf_op jit(solution)/shard_map/dot_general | solution.py:163
  148.3 0.3 fusion.17
  148.7 0.1 fusion.79
  148.8 0.2 copy.81
  149.0 0.2 copy.80
  149.2 2.0 subtract_convert_fusion
  151.1 1.8 copy.63
  152.9 1.8 copy.68
  154.7 4.6 %fusion.18 = bf16[4,256,256]{2,0,1:T(4,128)(2,1)S(1)} fusion(bf16[32,256,256]{2,1,0:T(8,128)(2,1)} %all-gather.5.cloned.1.call-done, s32[4]{0:T(128)S(1)} %dynamic-slice_reduce_fusion.1), kind=kOutput, calls=%fused_computation.24 | convolution fusion | flops 17039488 | bytes 4718608 | tf_op jit(solution)/shard_map/rj,jcd->rcd/dot_general | solution.py:184
  159.4 0.1 copy.61
  159.5 1.0 copy.62
  160.5 39.5 %all-gather.9.cloned.1.call-done = bf16[32,256,256]{2,1,0:T(8,128)(2,1)} async-done(((bf16[2,256,256]{2,1,0:T(8,128)(2,1)}), bf16[32,256,256]{2,1,0:T(8,128)(2,1)}) %all-gather.9.cloned.1.call-update) | async-done | bytes 4194320 | tf_op jit(solution)/shard_map/all_gather | solution.py:178
  200.0 4.7 %fusion.21 = bf16[4,256,256]{2,0,1:T(4,128)(2,1)S(1)} fusion(bf16[32,256,256]{2,1,0:T(8,128)(2,1)} %all-gather.9.cloned.1.call-done, s32[4]{0:T(128)S(1)} %dynamic-slice_reduce_fusion.1), kind=kOutput, calls=%fused_computation.25 | convolution fusion | flops 17039488 | bytes 4718608 | tf_op jit(solution)/shard_map/rj,jcd->rcd/dot_general | solution.py:183
  204.6 0.1 copy.67
  204.8 1.9 fusion.5
  206.7 2.2 fusion
  208.9 2.8 %divide_convert_fusion = bf16[512,1,2,256]{0,3,2,1:T(8,128)(2,1)S(1)} fusion(f32[2048,512,2]{1,0,2:T(8,128)S(1)} %get-tuple-element.25, f32[2,512]{1,0:T(2,128)S(1)} %get-tuple-element.24, pred[512,2048]{0,1:T(8,128)(4,1)S(1)} %copy-done.3, bf16[512,256]{0,1:T(8,128)(2,1)S(1)} %copy-done.6, bf16[512,256]{0,1:T(8,128)(2,1)S(1)} %copy-done.8, ...), kind=kOutput, calls=%fused_computation.42 | convolution fusion | flops 1085800448 | bytes 11018240 | tf_op jit(solution)/shard_map/krts,skd->tkrd/dot_general | solution.py:96
  211.7 3.9 %convolution_convert_fusion = bf16[512,3584]{0,1:T(8,128)(2,1)} fusion(bf16[512,512]{0,1:T(8,128)(2,1)S(1)} %bitcast.110, bf16[512,3584]{1,0:T(8,128)(2,1)S(1)} %copy-done.17), kind=kOutput, calls=%fused_computation.11 | convolution fusion | flops 1880883200 | bytes 7864320 | tf_op jit(solution)/shard_map/dot_general | solution.py:201
  215.7 36.6 %reduce-scatter.2.cloned.1.call-done = bf16[512,448]{0,1:T(8,128)(2,1)} async-done(((bf16[512,3584]{0,1:T(8,128)(2,1)}), bf16[512,448]{0,1:T(8,128)(2,1)}) %reduce-scatter.2.cloned.1.call-update) | async-done | bytes 458768 | tf_op jit(solution)/shard_map/reduce_scatter | solution.py:202
  (57 shorter events, 0.4 us)
Async XLA Ops:
  6.5 90.5 %copy-start = (bf16[3584,256]{1,0:T(8,128)(2,1)S(1)}, bf16[3584,256]{1,0:T(8,128)(2,1)}, u32[]{:S(2)}) copy-start(bf16[3584,256]{1,0:T(8,128)(2,1)} %param.20) | copy-start | bytes 5505028
  6.5 13.1 %copy-start.14 = (s32[16,4]{0,1:T(4,128)S(1)}, s32[16,4]{0,1:T(4,128)}, u32[]{:S(2)}) copy-start(s32[16,4]{0,1:T(4,128)} %param.26) | copy-start | bytes 772
  6.5 13.8 %copy-start.13 = (s32[16,4]{0,1:T(4,128)S(1)}, s32[16,4]{0,1:T(4,128)}, u32[]{:S(2)}) copy-start(s32[16,4]{0,1:T(4,128)} %param.24) | copy-start | bytes 772
  6.5 14.3 %copy-start.16 = (s32[16,4]{0,1:T(4,128)S(1)}, s32[16,4]{0,1:T(4,128)}, u32[]{:S(2)}) copy-start(s32[16,4]{0,1:T(4,128)} %param.29) | copy-start | bytes 772
  6.5 18.3 %copy-start.18 = (s32[16]{0:T(128)S(1)}, s32[16]{0:T(128)}, u32[]{:S(2)}) copy-start(s32[16]{0:T(128)} %param.27) | copy-start | bytes 196
  6.5 20.8 %copy-start.15 = (s32[16,4]{0,1:T(4,128)S(1)}, s32[16,4]{0,1:T(4,128)}, u32[]{:S(2)}) copy-start(s32[16,4]{0,1:T(4,128)} %param.28) | copy-start | bytes 772
  6.6 21.0 %copy-start.1 = (s32[64]{0:T(128)S(1)}, s32[64]{0:T(128)}, u32[]{:S(2)}) copy-start(s32[64]{0:T(128)} %param.25) | copy-start | bytes 772
  6.6 53.0 %all-gather.11.cloned.1.call-start = ((), (), s32[]{:S(2)}) async-start(), calls=%async_computation.5 | async-start | bytes 1114112 | tf_op jit(solution)/shard_map/all_gather | solution.py:143
  7.3 83.2 %all-gather.7.cloned.1.call-start = ((), (), s32[]{:S(2)}) async-start(), calls=%async_computation.3 | async-start | bytes 4128768 | tf_op jit(solution)/shard_map/all_gather | solution.py:128
  8.1 146.7 %all-gather.5.cloned.1.call-start = ((), (), s32[]{:S(2)}) async-start(), calls=%async_computation.2 | async-start | bytes 4456448 | tf_op jit(solution)/shard_map/all_gather | solution.py:179
  11.1 26.5 %all-to-all-start = ((bf16[16,4,16,448]{3,1,2,0:T(4,128)(2,1)}), bf16[16,4,16,448]{3,1,2,0:T(4,128)(2,1)S(1)}, u32[]{:S(2)}, u32[]{:S(2)}) async-start(bf16[16,4,16,448]{3,1,2,0:T(4,128)(2,1)} %stack.2), calls=%async_computation | async-start | bytes 2097152 | tf_op jit(solution)/shard_map/all_to_all | solution.py:13
  19.0 180.9 %all-gather.9.cloned.1.call-start = ((), (), s32[]{:S(2)}) async-start(), calls=%async_computation.4 | async-start | bytes 4456448 | tf_op jit(solution)/shard_map/all_gather | solution.py:178
  19.6 232.7 %reduce-scatter.2.cloned.1.call-start = ((), (), s32[]{:S(2)}) async-start(), calls=%async_computation.6 | async-start | bytes 4128768 | tf_op jit(solution)/shard_map/reduce_scatter | solution.py:202
  39.0 54.5 %copy-start.12 = (f32[3584]{0:T(1024)S(1)}, f32[3584]{0:T(1024)}, u32[]{:S(2)}) copy-start(f32[3584]{0:T(1024)} %param.17) | copy-start | bytes 43012
  90.5 3.1 %copy-start.2 = (bf16[512,3584]{0,1:T(8,128)(2,1)S(1)}, bf16[512,3584]{0,1:T(8,128)(2,1)}, u32[]{:S(2)}) copy-start(bf16[512,3584]{0,1:T(8,128)(2,1)} %all-gather.7.cloned.1.call-done) | copy-start | bytes 11010052
  95.2 1.8 copy-start.4
  100.7 50.4 %collective-permute-start = (bf16[512,256]{1,0:T(8,128)(2,1)}, bf16[512,256]{1,0:T(8,128)(2,1)}, u32[]{:S(2)}, u32[]{:S(2)}) collective-permute-start(bf16[512,256]{1,0:T(8,128)(2,1)} %convolution_convert_fusion.1), channel_id=1, source_target_pairs={{0,8},{8,16},{16,24},{24,32},{32,40},{40,48},{48,56},{56,64},{64,7... | collective-permute-start | bytes 786440 | tf_op jit(solution)/shard_map/ppermute | solution.py:21
  112.3 40.6 %collective-permute-start.1 = (bf16[512,256]{0,1:T(8,128)(2,1)}, bf16[512,256]{0,1:T(8,128)(2,1)}, u32[]{:S(2)}, u32[]{:S(2)}) collective-permute-start(bf16[512,256]{0,1:T(8,128)(2,1)} %maximum_bitcast_fusion.6), channel_id=1, source_target_pairs={{0,8},{8,16},{16,24},{24,32},{32,40},{40,48},{48,56},{56,64},{64,7... | collective-permute-start | bytes 786440 | tf_op jit(solution)/shard_map/ppermute | solution.py:21
  159.4 45.3 %copy-start.3 = (pred[512,2048]{0,1:T(8,128)(4,1)S(1)}, pred[512,2048]{0,1:T(8,128)(4,1)}, u32[]{:S(2)}) copy-start(pred[512,2048]{0,1:T(8,128)(4,1)} %pad_add_fusion) | copy-start | bytes 3145732
  160.5 44.2 %copy-start.7 = (bf16[512,256]{1,0:T(8,128)(2,1)S(1)}, bf16[512,256]{1,0:T(8,128)(2,1)}, u32[]{:S(2)}) copy-start(bf16[512,256]{1,0:T(8,128)(2,1)} %copy.69) | copy-start | bytes 786436
  160.5 44.3 %copy-start.9 = (bf16[512,256]{1,0:T(8,128)(2,1)S(1)}, bf16[512,256]{1,0:T(8,128)(2,1)}, u32[]{:S(2)}) copy-start(bf16[512,256]{1,0:T(8,128)(2,1)} %copy.68) | copy-start | bytes 786436
  200.0 4.8 %copy-start.10 = (bf16[512,2,128]{2,0,1:T(8,128)(2,1)S(1)}, bf16[512,2,128]{2,0,1:T(8,128)(2,1)}, u32[]{:S(2)}) copy-start(bf16[512,2,128]{2,0,1:T(8,128)(2,1)} %get-tuple-element.12) | copy-start | bytes 786436
  200.0 4.8 %copy-start.11 = (bf16[512,2,128]{2,0,1:T(8,128)(2,1)S(1)}, bf16[512,2,128]{2,0,1:T(8,128)(2,1)}, u32[]{:S(2)}) copy-start(bf16[512,2,128]{2,0,1:T(8,128)(2,1)} %get-tuple-element.13) | copy-start | bytes 786436
  206.6 2.2 copy-start.5
  206.6 2.2 copy-start.6
  206.7 2.2 copy-start.8
  208.9 2.8 %copy-start.17 = (bf16[512,3584]{1,0:T(8,128)(2,1)S(1)}, bf16[512,3584]{1,0:T(8,128)(2,1)}, u32[]{:S(2)}) copy-start(bf16[512,3584]{1,0:T(8,128)(2,1)} %param.21) | copy-start | bytes 11010052
Sparse Core Ops, SparseCore 0:
  9.5 49.9 all-gather.10
  61.2 29.2 all-gather.6
  92.6 53.9 all-gather.4
  148.7 51.2 all-gather.8
  215.8 36.4 reduce-scatter.1
